TPU v7x, 32 devices: a whole 2x2x4 slice. The times are simulated.
32 devices in a mesh: grp: 2 (over y), wide: 4 (over z), col: 2 (over x), inc: 2 (over core).
Axes of the slice: x: 2, y: 2, z: 4, core: 2. Of those that a mesh axis runs over, the one named last changes fastest.
Arguments:
- values_in: bfloat16 [32, 64, 256, 512], P(('grp', 'col'), 'inc', 'wide'), parts along dimension 0, may hold values from -6 to 6
- shock_load: float32 [32], P(('grp', 'col')), parts along dimension 0, may hold values from -4 to 4
- price_field: float32 [128, 256, 512], P(('grp', 'inc'), 'wide'), parts along dimension 0, may hold values from -6 to 6
- rate_liquid: float32 [128, 256, 512], P(('grp', 'inc'), 'wide'), parts along dimension 0, may hold values from 0.05 to 0.5
- rate_illiquid: float32 [128, 256, 512], P(('grp', 'inc'), 'wide'), parts along dimension 0, may hold values from 0.05 to 0.5
- mask_liquid: int32 [128, 256, 512], P(('grp', 'inc'), 'wide'), parts along dimension 0, may hold values 0 or 1
- mask_illiquid: int32 [128, 256, 512], P(('grp', 'inc'), 'wide'), parts along dimension 0, may hold values 0 or 1
- jump_inverse: float32 [128, 64], P('grp'), parts along dimension 0, may hold values from -0.07 to 0.87
- coef_liquid: int32 [4096], replicated, may hold values from 0 to 127, as said below
- coef_illiquid: int32 [4096], replicated, may hold values from 0 to 255
- coef_income: int32 [4096], replicated, may hold values from 0 to 63
- owner: int32 [4096], replicated, may hold values from 0 to 7, as said below
Outputs:
- reduced: float32 [32, 8192], P(('grp', 'col'), ('wide', 'inc')), parts along dimension 0
There are 2 independent parts, one for each index of `grp`. A program takes and returns all parts, laid end to end along the dimension named above; an argument that names none is the same for every part. Nothing has to cross between parts.
Inputs may be any that keep to these rules, and one draw needn't show every extreme that they name: `coef_liquid`: every retained coefficient has liquid frequency below 128. No owner has more than 1024 rows, and some owner has exactly 1024.
All inputs are finite; a program needn't handle non-finite values. No bound on the sum of `mask_liquid` or of `mask_illiquid` on one device may be relied on, other than what follows from the above.
Results may differ from a plain program's by a relative error of at most 0.0003.
Values may be sent and summed in bfloat16 or wider, within the bound.
No kernel may reach another device: no remote copies, remote signals or barrier semaphores. Data moves between devices by JAX's collectives and lax.ppermute only.
A program may use at most 256 MiB of HBM per device.

v0:
```python
import jax
import jax.numpy as jnp
from jax import lax
from jax.sharding import PartitionSpec as P

NB = 512
NA = 256
NZ = 64
KBLOW = 128


def padded_2(cells, sides, width):
    for axis, dim in sides:
        count = lax.axis_size(axis)
        ends = count - 1
        head = lax.slice_in_dim(cells, 0, width, axis=dim)
        tail = lax.slice_in_dim(cells, cells.shape[dim] - width, cells.shape[dim], axis=dim)
        cells = jnp.concatenate(
            [
                lax.ppermute(tail, axis, [(i, (i + 1) % count) for i in range(ends)]),
                cells,
                lax.ppermute(head, axis, [((i + 1) % count, i) for i in range(ends)]),
            ],
            axis=dim,
        )
    return cells


def cosine_table(count):
    freq = jnp.arange(count, dtype=jnp.int32)[:, None]
    cell = jnp.arange(count, dtype=jnp.int32)[None, :]
    phase = (2 * cell + 1) * freq % (4 * count)
    angle = jnp.pi * phase.astype(jnp.float32) / (2.0 * count)
    first = jnp.where(freq == 0, jnp.sqrt(jnp.float32(0.5)), jnp.float32(1.0))
    return jnp.cos(angle) * jnp.sqrt(jnp.float32(2.0 / count)) * first


def slot_targets(owner, owners, capacity):
    onehot = (owner[:, None] == jnp.arange(owners, dtype=jnp.int32)[None, :]).astype(jnp.int32)
    before = jnp.cumsum(onehot, axis=0) - onehot
    slot = jnp.sum(before * onehot, axis=1)
    return owner * capacity + slot


def body(
    values_in,
    shock_load,
    price_field,
    rate_liquid,
    rate_illiquid,
    mask_liquid,
    mask_illiquid,
    jump_inverse,
    coef_liquid,
    coef_illiquid,
    coef_income,
    owner,
):
    high = lax.Precision.HIGH
    columns, nz_loc, na_loc, _ = values_in.shape
    wide_pos = lax.axis_index("wide")
    inc_pos = lax.axis_index("inc")
    wide_count = lax.axis_size("wide")
    padded = padded_2(values_in, (("wide", 2),), 1).astype(jnp.float32)
    center = padded[:, :, 1:-1]
    lower = jnp.where(wide_pos == 0, center[:, :, 0:1], padded[:, :, 0:1])
    upper = jnp.where(wide_pos == wide_count - 1, center[:, :, -1:], padded[:, :, -1:])
    fwd_a = jnp.concatenate([center[:, :, 1:], upper], axis=2) - center
    bwd_a = center - jnp.concatenate([lower, center[:, :, :-1]], axis=2)
    step_b = center[:, :, :, 1:] - center[:, :, :, :-1]
    zero_b = jnp.zeros(center.shape[:3] + (1,), jnp.float32)
    fwd_b = jnp.concatenate([step_b, zero_b], axis=3)
    bwd_b = jnp.concatenate([zero_b, step_b], axis=3)
    mask_b = mask_liquid.astype(jnp.float32)
    mask_a = mask_illiquid.astype(jnp.float32)
    load = shock_load[:, None, None, None]
    explicit = (
        center
        + rate_liquid * (mask_b * fwd_b - (1.0 - mask_b) * bwd_b)
        + rate_illiquid * (mask_a * fwd_a - (1.0 - mask_a) * bwd_a)
        + load * price_field
    )
    table_b = cosine_table(NB)[:KBLOW]
    liquid_part = jnp.einsum("kb,czab->czak", table_b, explicit, precision=high)
    table_a = lax.dynamic_slice_in_dim(cosine_table(NA), wide_pos * na_loc, na_loc, axis=1)
    illiquid_part = jnp.einsum("ja,czak->jkcz", table_a, liquid_part, precision=high)
    rows = illiquid_part.reshape(NA * KBLOW, columns * nz_loc)
    picked = jnp.take(rows, coef_illiquid * KBLOW + coef_liquid, axis=0)
    folded = jnp.dot(cosine_table(NZ), jump_inverse, precision=lax.Precision.HIGHEST)
    folded = lax.dynamic_slice_in_dim(folded, inc_pos * nz_loc, nz_loc, axis=1)
    weight = jnp.take(folded, coef_income, axis=0)
    partial = jnp.sum(picked.reshape(-1, columns, nz_loc) * weight[:, None, :], axis=2)
    kept = lax.psum(partial, ("wide", "inc"))
    owners = lax.axis_size(("wide", "inc"))
    count = owner.shape[0]
    capacity = 2 * count // owners
    targets = slot_targets(owner, owners, capacity)
    source = (
        jnp.full((owners * capacity,), count, jnp.int32)
        .at[targets]
        .set(jnp.arange(count, dtype=jnp.int32))
    )
    mine = lax.dynamic_slice_in_dim(source, lax.axis_index(("wide", "inc")) * capacity, capacity)
    gathered = jnp.take(kept, jnp.minimum(mine, count - 1), axis=0)
    return jnp.where((mine < count)[None, :], gathered.T, jnp.float32(0.0))


def solution(mesh):
    placed = (
        P(("grp", "col"), "inc", "wide", None),
        P(("grp", "col")),
        P(("grp", "inc"), "wide", None),
        P(("grp", "inc"), "wide", None),
        P(("grp", "inc"), "wide", None),
        P(("grp", "inc"), "wide", None),
        P(("grp", "inc"), "wide", None),
        P("grp", None),
        P(),
        P(),
        P(),
        P(),
    )
    return jax.shard_map(
        body,
        mesh=mesh,
        in_specs=placed,
        out_specs=P(("grp", "col"), ("wide", "inc")),
        check_vma=False,
    )
```

profile of v0, /device:TPU:0, one launch (start us, length us, event | category | flops | bytes accessed | tf_op | source)
XLA Modules:
  0.0 500.5 jit_solution(14844286475312916411)
XLA Ops:
  6.6 3.3 fusion.94
  9.9 5.6 %collective-permute-start = (bf16[8,32,1,512]{3,1,2,0:T(8,128)(2,1)S(1)}, bf16[8,32,1,512]{3,1,2,0:T(8,128)(2,1)}, u32[]{:S(2)}, u32[]{:S(2)}) collective-permute-start(bf16[8,32,1,512]{3,1,2,0:T(8,128)(2,1)S(1)} %copy.34), channel_id=1, source_target_pairs={{0,4},{4,8},{8,12},{1,5},{5,9},{9,13},{2,6},{6,10},{10,14},{3,7},{... | collective-permute-start | bytes 786440 | tf_op jit(solution)/shard_map/ppermute | solution.py:20
  15.6 0.7 copy.35
  16.3 1.3 collective-permute-start.1
  17.6 4.9 convert_element_type.28
  22.6 8.5 %broadcast_subtract_fusion = (f32[32,64,512]{2,1,0:T(8,128)}, f32[32,64,512]{2,1,0:T(8,128)}) fusion(s32[32,64,512]{2,1,0:T(8,128)} %param.18, s32[32,64,512]{2,1,0:T(8,128)} %param.17), kind=kLoop, calls=%fused_computation.39 | loop fusion | flops 4194304 | bytes 16777216 | tf_op jit(solution)/shard_map/sub | solution.py:80
  31.1 4.9 convert_element_type.29
  36.0 0.8 broadcast_compare_fusion.3
  36.9 0.9 negate_select_fusion.2
  40.3 14.1 %gather_fusion.1 = f32[4096,32]{1,0:T(8,128)} fusion(f32[64,32]{1,0:T(8,128)S(1)} %copy.28, s32[4096]{0:T(1024)S(1)} %fusion.78), kind=kCustom, calls=%fused_computation.1 | custom fusion | bytes 1064960 | tf_op jit(solution)/shard_map/jit(_take)/gather | solution.py:91
  54.4 3.6 broadcast_select_fusion
  58.0 1.4 copy.29
  59.4 2.3 reduce-window.6
  62.5 15.5 %scatter_custom_fusion = s32[8192]{0:T(1024)S(1)} fusion(s32[4096]{0:T(1024)S(1)} %compare_select_fusion.2, s32[4096]{0:T(1024)S(1)} %iota.47, s32[]{:T(128)} %constant.66.clone.1), kind=kCustom, calls=%fused_computation.109 | custom fusion | bytes 32772 | tf_op jit(solution)/shard_map/scatter | solution.py:101
  79.2 1.4 copy.23
  80.6 1.4 copy.24
  82.0 20.9 %maximum_convert_fusion = f32[8,32,66,512]{3,2,1,0:T(8,128)} fusion(bf16[8,32,1,512]{3,2,1,0:T(2,128)(2,1)S(1)} %copy.24, bf16[8,32,64,512]{3,2,1,0:T(8,128)(2,1)} %param.12, bf16[8,32,1,512]{3,2,1,0:T(2,128)(2,1)S(1)} %copy.23), kind=kLoop, calls=%fused_computation.28 | loop fusion | flops 51904512 | bytes 51904512 | tf_op jit(solution)/shard_map/convert_element_type | solution.py:64
  102.9 47.7 %fusion.93 = (f32[8,32,63,512]{3,2,1,0:T(8,128)}, f32[8,32,63,512]{3,2,1,0:T(8,128)}) fusion(f32[8,32,66,512]{3,2,1,0:T(8,128)} %maximum_convert_fusion), kind=kLoop, calls=%fused_computation.140 | loop fusion | bytes 132120576 | tf_op jit(solution)/shard_map/slice | solution.py:69
  150.6 36.7 %slice_subtract_fusion = f32[8,32,64,511]{3,2,1,0:T(8,128)} fusion(f32[8,32,66,512]{3,2,1,0:T(8,128)} %maximum_convert_fusion), kind=kLoop, calls=%fused_computation.5 | loop fusion | flops 8372224 | bytes 100466688 | tf_op jit(solution)/shard_map/sub | solution.py:70
  187.3 4.8 broadcast_select_fusion.1
  192.2 73.0 %fusion.5 = f32[8,32,64,128]{3,2,1,0:T(8,128)} fusion(f32[8,32,1,512]{3,2,1,0:T(1,128)S(1)} %get-tuple-element.8, f32[8,32,63,512]{3,2,1,0:T(8,128)} %get-tuple-element.6, f32[8,32,63,512]{3,2,1,0:T(8,128)} %get-tuple-element.5, f32[8,32,1,512]{3,2,1,0:T(1,128)S(1)} %get-tuple-element.7, f32[8,32,66,512]{3,2,1,0:T(8,128)} %maximum_convert_fusion, ...), kind=kOutput, calls=%fused_computation.12 | convolution fusion | flops 6577061888 | bytes 173409280 | tf_op jit(solution)/shard_map/kb,czab->czak/dot_general | solution.py:84
  265.2 22.0 %convolution_bitcast_fusion = f32[256,128,8,32]{0,1,3,2:T(8,128)} fusion(f32[8,32,64,128]{3,2,1,0:T(8,128)} %fusion.5, s32[256,256]{0,1:T(8,128)} %negate_select_fusion.2, s32[]{:T(128)S(6)} %select_n.124, pred[256,256]{0,1:T(32,128)(4,1)} %get-tuple-element.16, pred[256,256]{0,1:T(32,128)(4,1)} %get-tuple-element.15, f32[256]{0:T(256)S(1)} %copy-done.14), kind=kOutput, calls=%fused_computation.37 | convolution fusion | flops 3221323776 | bytes 42042372 | tf_op jit(solution)/shard_map/ja,czak->jkcz/dot_general | solution.py:86
  287.3 31.1 %copy.25 = f32[256,128,8,32]{1,0,3,2:T(8,128)} copy(f32[256,128,8,32]{0,1,3,2:T(8,128)} %convolution_bitcast_fusion) | data formatting | bytes 67108864 | tf_op jit(solution)/shard_map/ja,czak->jkcz/transpose | solution.py:86
  318.4 31.8 %copy.40 = f32[32,8,256,128]{3,1,2,0:T(8,128)} copy(f32[32,8,256,128]{3,2,1,0:T(8,128)} %bitcast.48) | data formatting | bytes 67108864
  350.1 33.4 %copy.26 = f32[32768,256]{1,0:T(8,128)} copy(f32[32768,256]{0,1:T(8,128)} %bitcast.49) | data formatting | bytes 67108864 | tf_op jit(solution)/shard_map/reshape | solution.py:87
  383.6 26.7 %gather_fusion = f32[4096,256]{1,0:T(8,128)} fusion(f32[32768,256]{1,0:T(8,128)} %copy.26, s32[4096]{0:T(1024)S(1)} %copy-done.5), kind=kCustom, calls=%fused_computation | custom fusion | bytes 8404992 | tf_op jit(solution)/shard_map/jit(_take)/gather | solution.py:88
  410.3 5.6 %copy.27 = f32[4096,256]{0,1:T(8,128)} copy(f32[4096,256]{1,0:T(8,128)} %gather_fusion) | data formatting | bytes 8388608 | tf_op jit(solution)/shard_map/jit(_take)/gather | solution.py:88
  415.9 2.9 multiply_reduce_fusion
  418.8 1.9 copy.30
  421.5 66.6 %all-reduce.4.cloned.1.call-done = f32[4096,8]{1,0:T(8,128)} async-done(((f32[4096,8]{1,0:T(8,128)}), f32[4096,8]{1,0:T(8,128)}) %all-reduce.4.cloned.1.call-update) | async-done | bytes 131088 | tf_op jit(solution)/shard_map/psum | solution.py:93
  488.1 4.4 gather_fusion.2
  492.8 0.8 copy.31
  (62 shorter events, 5.6 us)
Async XLA Ops:
  6.5 33.3 %copy-start = (f32[64,64]{1,0:T(8,128)S(1)}, f32[64,64]{1,0:T(8,128)}, u32[]{:S(2)}) copy-start(f32[64,64]{1,0:T(8,128)} %param.19) | copy-start | bytes 49156
  6.5 31.8 %copy-start.8 = (s32[4096]{0:T(1024)S(1)}, s32[4096]{0:T(1024)}, u32[]{:S(2)}) copy-start(s32[4096]{0:T(1024)} %param.22) | copy-start | bytes 49156
  6.5 31.8 %copy-start.6 = (s32[4096]{0:T(1024)S(1)}, s32[4096]{0:T(1024)}, u32[]{:S(2)}) copy-start(s32[4096]{0:T(1024)} %param.20) | copy-start | bytes 49156
  6.5 31.8 %copy-start.7 = (s32[4096]{0:T(1024)S(1)}, s32[4096]{0:T(1024)}, u32[]{:S(2)}) copy-start(s32[4096]{0:T(1024)} %param.21) | copy-start | bytes 49156
  6.5 52.9 %copy-start.4 = (s32[4096]{0:T(1024)S(1)}, s32[4096]{0:T(1024)}, u32[]{:S(2)}) copy-start(s32[4096]{0:T(1024)} %param.23) | copy-start | bytes 49156
  6.5 481.5 %all-reduce.4.cloned.1.call-start = ((), (), s32[]{:S(2)}) async-start(), calls=%async_computation | async-start | bytes 4194304 | tf_op jit(solution)/shard_map/psum | solution.py:93
  9.9 69.3 %collective-permute-start = (bf16[8,32,1,512]{3,1,2,0:T(8,128)(2,1)S(1)}, bf16[8,32,1,512]{3,1,2,0:T(8,128)(2,1)}, u32[]{:S(2)}, u32[]{:S(2)}) collective-permute-start(bf16[8,32,1,512]{3,1,2,0:T(8,128)(2,1)S(1)} %copy.34), channel_id=1, source_target_pairs={{0,4},{4,8},{8,12},{1,5},{5,9},{9,13},{2,6},{6,10},{10,14},{3,7},{... | collective-permute-start | bytes 786440 | tf_op jit(solution)/shard_map/ppermute | solution.py:20
  16.3 64.3 %collective-permute-start.1 = (bf16[8,32,1,512]{3,1,2,0:T(8,128)(2,1)}, bf16[8,32,1,512]{3,1,2,0:T(8,128)(2,1)}, u32[]{:S(2)}, u32[]{:S(2)}) collective-permute-start(bf16[8,32,1,512]{3,1,2,0:T(8,128)(2,1)} %copy.35), channel_id=1, source_target_pairs={{4,0},{8,4},{12,8},{5,1},{9,5},{13,9},{6,2},{10,6},{14,10},{7,3},{... | collective-permute-start | bytes 786440 | tf_op jit(solution)/shard_map/ppermute | solution.py:22
  36.0 66.9 %copy-start.13 = (f32[512]{0:T(512)}, f32[512]{0:T(512)S(1)}, u32[]{:S(2)}) copy-start(f32[512]{0:T(512)S(1)} %select_multiply_fusion) | copy-start | bytes 6148
  78.0 72.6 %copy-start.9 = (s32[8192]{0:T(1024)}, s32[8192]{0:T(1024)S(1)}, u32[]{:S(2)}) copy-start(s32[8192]{0:T(1024)S(1)} %scatter_custom_fusion) | copy-start | bytes 98308
  150.6 41.6 %copy-start.10 = (f32[8]{0:T(128)S(1)}, f32[8]{0:T(128)}, u32[]{:S(2)}) copy-start(f32[8]{0:T(128)} %param.13) | copy-start | bytes 100
  150.6 41.6 %slice-start = ((f32[512]{0:T(512)}), f32[128]{0:T(128)S(1)}, s32[]{:S(2)}) async-start(f32[512]{0:T(512)} %copy-done.13), calls=%async_computation.1 | async-start | bytes 1024 | tf_op jit(solution)/shard_map/slice | solution.py:83
  187.3 4.9 copy-start.2
  192.2 73.0 %copy-start.14 = (f32[256]{0:T(256)S(1)}, f32[256]{0:T(256)}, u32[]{:S(2)}) copy-start(f32[256]{0:T(256)} %fusion.80) | copy-start | bytes 3076
  350.1 33.4 %copy-start.5 = (s32[4096]{0:T(1024)S(1)}, s32[4096]{0:T(1024)}, u32[]{:S(2)}) copy-start(s32[4096]{0:T(1024)} %broadcast_clamp_fusion) | copy-start | bytes 49156
  350.1 143.5 %copy-start.1 = (f32[64,64]{1,0:T(8,128)S(1)}, f32[64,64]{1,0:T(8,128)}, u32[]{:S(2)}) copy-start(f32[64,64]{1,0:T(8,128)} %param.19) | copy-start | bytes 49156
  383.6 32.3 %copy-start.3 = (f32[4096,32]{0,1:T(8,128)S(1)}, f32[4096,32]{0,1:T(8,128)}, u32[]{:S(2)}) copy-start(f32[4096,32]{0,1:T(8,128)} %copy.29) | copy-start | bytes 1572868
  383.6 32.3 %copy-start.11 = (pred[4096]{0:T(1024)(128)(4,1)S(1)}, pred[4096]{0:T(1024)(128)(4,1)}, u32[]{:S(2)}) copy-start(pred[4096]{0:T(1024)(128)(4,1)} %compare_and_fusion.1) | copy-start | bytes 12292
  383.6 104.5 %copy-start.12 = (s32[1024]{0:T(1024)S(1)}, s32[1024]{0:T(1024)}, u32[]{:S(2)}) copy-start(s32[1024]{0:T(1024)} %fusion.79) | copy-start | bytes 12292
Sparse Core Ops, SparseCore 0:
  420.9 67.1 all-reduce.3
where the time goes:
time: 502 us; the launch traced here: 500 us
  local copies, waits for them, and re-layouts  222 us (44%)
  other arithmetic  96.1 us (19%)
  matrix products  95.4 us (19%)
  waiting for transfers between devices  66.7 us (13%)
  between operations  13.7 us (3%)
  starting transfers between devices  6.96 us (1%)
    dot_general x1, matrix products, body(): liquid_part = jnp.einsum('kb,czab->czak', table_b, explicit, precision=high)  73 us
    psum x1, waiting for transfers between devices, body(): kept = lax.psum(partial, ('wide', 'inc'))  66.6 us
    slice x1, local copies, waits for them, and re-layouts, body(): bwd_a = center - jnp.concatenate([lower, center[:, :, :-1]], axis=2)  47.7 us
    sub x1, other arithmetic, body(): step_b = center[:, :, :, 1:] - center[:, :, :, :-1]  36.7 us
    reshape x1, local copies, waits for them, and re-layouts, body(): rows = illiquid_part.reshape(NA * KBLOW, columns * nz_loc)  33.4 us
    unnamed x33, local copies, waits for them, and re-layouts  32.6 us
    gather x2, local copies, waits for them, and re-layouts, body(): picked = jnp.take(rows, coef_illiquid * KBLOW + coef_liquid, axis=0)  32.3 us
    transpose x1, local copies, waits for them, and re-layouts, body(): jnp.einsum('ja,czak->jkcz', table_a, liquid_part, precision=high)  31.1 us
  transfers between devices with their start and end apart: 3, of which 1 were waited for; matrix products, arithmetic and copies ran while one was open for 13% of the time, Pallas kernels for 0%

commit v1 on v0

--- a/solution.py
+++ b/solution.py
@@ -90,7 +90,7 @@
     folded = lax.dynamic_slice_in_dim(folded, inc_pos * nz_loc, nz_loc, axis=1)
     weight = jnp.take(folded, coef_income, axis=0)
     partial = jnp.sum(picked.reshape(-1, columns, nz_loc) * weight[:, None, :], axis=2)
-    kept = lax.psum(partial, ("wide", "inc"))
+    kept = jnp.sum(lax.all_gather(partial, ("wide", "inc")), axis=0)
     owners = lax.axis_size(("wide", "inc"))
     count = owner.shape[0]
     capacity = 2 * count // owners

time: 502 us -> 439 us (0.87)
  waiting for transfers between devices: 66.7 us -> 5.96 us
    psum x1 -> x0, waiting for transfers between devices: 66.6 us -> none  [body(): kept = lax.psum(partial, ('wide', 'inc'))]
    all_gather x0 -> x1, waiting for transfers between devices: none -> 5.94 us  [body(): kept = jnp.sum(lax.all_gather(partial, ('wide', 'inc')), axis=0)]
    unnamed x33 -> x29, local copies, waits for them, and re-layouts: 32.6 us -> 32.6 us
  transfers between devices with their start and end apart: 3 -> 3, of which waited for: 1 -> 1; matrix products, arithmetic and copies ran while one was open for 13% -> 14% of each run, Pallas kernels for 0% -> 0%
where the time goes in v1:
time: 439 us; the launch traced here: 437 us
  local copies, waits for them, and re-layouts  219 us (50%)
  other arithmetic  96.4 us (22%)
  matrix products  95.4 us (22%)
  between operations  13.7 us (3%)
  starting transfers between devices  6.95 us (2%)
  waiting for transfers between devices  5.96 us (1%)
    dot_general x1, matrix products, body(): liquid_part = jnp.einsum('kb,czab->czak', table_b, explicit, precision=high)  73.2 us
    slice x1, local copies, waits for them, and re-layouts, body(): bwd_a = center - jnp.concatenate([lower, center[:, :, :-1]], axis=2)  47.7 us
    sub x1, other arithmetic, body(): step_b = center[:, :, :, 1:] - center[:, :, :, :-1]  36.6 us
    reshape x1, local copies, waits for them, and re-layouts, body(): rows = illiquid_part.reshape(NA * KBLOW, columns * nz_loc)  33.5 us
    unnamed x29, local copies, waits for them, and re-layouts  32.6 us
    gather x2, local copies, waits for them, and re-layouts, body(): picked = jnp.take(rows, coef_illiquid * KBLOW + coef_liquid, axis=0)  32.3 us
    transpose x1, local copies, waits for them, and re-layouts, body(): jnp.einsum('ja,czak->jkcz', table_a, liquid_part, precision=high)  31.1 us
    dot_general x1, matrix products, body(): jnp.einsum('ja,czak->jkcz', table_a, liquid_part, precision=high)  21.8 us
  transfers between devices with their start and end apart: 3, of which 1 were waited for; matrix products, arithmetic and copies ran while one was open for 14% of the time, Pallas kernels for 0%

profile of v1, /device:TPU:0, one launch (start us, length us, event | category | flops | bytes accessed | tf_op | source)
XLA Modules:
  0.0 437.2 jit_solution(11128426106438819906)
XLA Ops:
  6.6 3.3 fusion.94
  9.9 5.6 %collective-permute-start = (bf16[8,32,1,512]{3,1,2,0:T(8,128)(2,1)S(1)}, bf16[8,32,1,512]{3,1,2,0:T(8,128)(2,1)}, u32[]{:S(2)}, u32[]{:S(2)}) collective-permute-start(bf16[8,32,1,512]{3,1,2,0:T(8,128)(2,1)S(1)} %copy.44), channel_id=1, source_target_pairs={{0,4},{4,8},{8,12},{1,5},{5,9},{9,13},{2,6},{6,10},{10,14},{3,7},{... | collective-permute-start | bytes 786440 | tf_op jit(solution)/shard_map/ppermute | solution.py:20
  15.5 0.7 copy.45
  16.3 1.3 collective-permute-start.1
  17.6 4.9 %convert_element_type.28 = f32[32,64,512]{2,1,0:T(8,128)} convert(s32[32,64,512]{2,1,0:T(8,128)} %param.17) | non-fusion elementwise | flops 1048576 | bytes 8388608 | tf_op jit(solution)/shard_map/convert_element_type | solution.py:74
  22.5 8.5 %broadcast_subtract_fusion = (f32[32,64,512]{2,1,0:T(8,128)}, f32[32,64,512]{2,1,0:T(8,128)}) fusion(s32[32,64,512]{2,1,0:T(8,128)} %param.18, s32[32,64,512]{2,1,0:T(8,128)} %param.17), kind=kLoop, calls=%fused_computation.39 | loop fusion | flops 4194304 | bytes 16777216 | tf_op jit(solution)/shard_map/sub | solution.py:80
  31.1 4.9 %convert_element_type.29 = f32[32,64,512]{2,1,0:T(8,128)} convert(s32[32,64,512]{2,1,0:T(8,128)} %param.18) | non-fusion elementwise | flops 1048576 | bytes 8388608 | tf_op jit(solution)/shard_map/convert_element_type | solution.py:75
  36.0 0.9 broadcast_compare_fusion.3
  36.9 0.8 negate_select_fusion.2
  40.3 14.1 %gather_fusion.1 = f32[4096,32]{1,0:T(8,128)} fusion(f32[64,32]{1,0:T(8,128)S(1)} %copy.38, s32[4096]{0:T(1024)S(1)} %fusion.78), kind=kCustom, calls=%fused_computation.1 | custom fusion | bytes 1064960 | tf_op jit(solution)/shard_map/jit(_take)/gather | solution.py:91
  54.3 3.6 broadcast_select_fusion
  57.9 1.4 copy.39
  59.9 1.4 copy.33
  61.3 1.4 copy.34
  62.7 20.7 %maximum_convert_fusion = f32[8,32,66,512]{3,2,1,0:T(8,128)} fusion(bf16[8,32,1,512]{3,2,1,0:T(2,128)(2,1)S(1)} %copy.34, bf16[8,32,64,512]{3,2,1,0:T(8,128)(2,1)} %param.12, bf16[8,32,1,512]{3,2,1,0:T(2,128)(2,1)S(1)} %copy.33), kind=kLoop, calls=%fused_computation.28 | loop fusion | flops 51904512 | bytes 51904512 | tf_op jit(solution)/shard_map/convert_element_type | solution.py:64
  83.5 47.7 %fusion.93 = (f32[8,32,63,512]{3,2,1,0:T(8,128)}, f32[8,32,63,512]{3,2,1,0:T(8,128)}) fusion(f32[8,32,66,512]{3,2,1,0:T(8,128)} %maximum_convert_fusion), kind=kLoop, calls=%fused_computation.140 | loop fusion | bytes 132120576 | tf_op jit(solution)/shard_map/slice | solution.py:69
  131.2 36.6 %slice_subtract_fusion = f32[8,32,64,511]{3,2,1,0:T(8,128)} fusion(f32[8,32,66,512]{3,2,1,0:T(8,128)} %maximum_convert_fusion), kind=kLoop, calls=%fused_computation.5 | loop fusion | flops 8372224 | bytes 100466688 | tf_op jit(solution)/shard_map/sub | solution.py:70
  167.8 4.8 %broadcast_select_fusion.1 = (f32[8,32,1,512]{3,2,1,0:T(1,128)S(1)}, f32[8,32,1,512]{3,2,1,0:T(1,128)S(1)}) fusion(pred[]{:T(512)S(6)} %eq.76, bf16[8,32,1,512]{3,2,1,0:T(2,128)(2,1)S(1)} %copy.34, bf16[8,32,64,512]{3,2,1,0:T(8,128)(2,1)} %param.12, bf16[8,32,1,512]{3,2,1,0:T(2,128)(2,1)S(1)} %copy.33, pred[]{:T(512)S(6)} %eq.75), kind=kLoop, calls=%fused_computation.45 | loop fusion | flops 3407872 | bytes 18350082 | tf_op jit(solution)/shard_map/jit(_where)/select_n | solution.py:66
  172.7 73.2 %fusion.5 = f32[8,32,64,128]{3,2,1,0:T(8,128)} fusion(f32[8,32,1,512]{3,2,1,0:T(1,128)S(1)} %get-tuple-element.8, f32[8,32,63,512]{3,2,1,0:T(8,128)} %get-tuple-element.6, f32[8,32,63,512]{3,2,1,0:T(8,128)} %get-tuple-element.5, f32[8,32,1,512]{3,2,1,0:T(1,128)S(1)} %get-tuple-element.7, f32[8,32,66,512]{3,2,1,0:T(8,128)} %maximum_convert_fusion, ...), kind=kOutput, calls=%fused_computation.12 | convolution fusion | flops 6577061888 | bytes 173409280 | tf_op jit(solution)/shard_map/kb,czab->czak/dot_general | solution.py:84
  245.9 21.8 %convolution_bitcast_fusion = f32[256,128,8,32]{0,1,3,2:T(8,128)} fusion(f32[8,32,64,128]{3,2,1,0:T(8,128)} %fusion.5, s32[256,256]{0,1:T(8,128)} %negate_select_fusion.2, s32[]{:T(128)S(6)} %select_n.124, pred[256,256]{0,1:T(32,128)(4,1)} %get-tuple-element.16, pred[256,256]{0,1:T(32,128)(4,1)} %get-tuple-element.15, f32[256]{0:T(256)S(1)} %copy-done.12), kind=kOutput, calls=%fused_computation.37 | convolution fusion | flops 3221323776 | bytes 42042372 | tf_op jit(solution)/shard_map/ja,czak->jkcz/dot_general | solution.py:86
  267.7 31.1 %copy.35 = f32[256,128,8,32]{1,0,3,2:T(8,128)} copy(f32[256,128,8,32]{0,1,3,2:T(8,128)} %convolution_bitcast_fusion) | data formatting | bytes 67108864 | tf_op jit(solution)/shard_map/ja,czak->jkcz/transpose | solution.py:86
  298.8 31.7 %copy.50 = f32[32,8,256,128]{3,1,2,0:T(8,128)} copy(f32[32,8,256,128]{3,2,1,0:T(8,128)} %bitcast.49) | data formatting | bytes 67108864
  330.5 33.5 %copy.36 = f32[32768,256]{1,0:T(8,128)} copy(f32[32768,256]{0,1:T(8,128)} %bitcast.50) | data formatting | bytes 67108864 | tf_op jit(solution)/shard_map/reshape | solution.py:87
  364.0 26.7 %gather_fusion = f32[4096,256]{1,0:T(8,128)} fusion(f32[32768,256]{1,0:T(8,128)} %copy.36, s32[4096]{0:T(1024)S(1)} %copy-done.5), kind=kCustom, calls=%fused_computation | custom fusion | bytes 8404992 | tf_op jit(solution)/shard_map/jit(_take)/gather | solution.py:88
  390.7 5.6 %copy.37 = f32[4096,256]{0,1:T(8,128)} copy(f32[4096,256]{1,0:T(8,128)} %gather_fusion) | data formatting | bytes 8388608 | tf_op jit(solution)/shard_map/jit(_take)/gather | solution.py:88
  396.3 3.5 multiply_reduce_fusion
  399.9 2.3 reduce-window.6
  403.0 15.5 %scatter_custom_fusion = s32[8192]{0:T(1024)S(1)} fusion(s32[4096]{0:T(1024)S(1)} %compare_select_fusion.2, s32[4096]{0:T(1024)S(1)} %iota.47, s32[]{:T(128)} %constant.66.clone.1), kind=kCustom, calls=%fused_computation.109 | custom fusion | bytes 32772 | tf_op jit(solution)/shard_map/scatter | solution.py:101
  418.6 5.9 %all-gather.3.cloned.1.call-done = f32[32768,8]{0,1:T(8,128)} async-done(((f32[4096,8]{0,1:T(8,128)}), f32[32768,8]{0,1:T(8,128)}) %all-gather.3.cloned.1.call-update) | async-done | bytes 1048592 | tf_op jit(solution)/shard_map/all_gather | solution.py:93
  424.5 1.3 reduce_sum.29
  426.4 2.8 gather_fusion.2
  429.6 0.8 copy.41
  (59 shorter events, 4.9 us)
Async XLA Ops:
  6.5 33.3 %copy-start = (f32[64,64]{1,0:T(8,128)S(1)}, f32[64,64]{1,0:T(8,128)}, u32[]{:S(2)}) copy-start(f32[64,64]{1,0:T(8,128)} %param.19) | copy-start | bytes 49156
  6.5 31.8 %copy-start.8 = (s32[4096]{0:T(1024)S(1)}, s32[4096]{0:T(1024)}, u32[]{:S(2)}) copy-start(s32[4096]{0:T(1024)} %param.22) | copy-start | bytes 49156
  6.5 31.8 %copy-start.6 = (s32[4096]{0:T(1024)S(1)}, s32[4096]{0:T(1024)}, u32[]{:S(2)}) copy-start(s32[4096]{0:T(1024)} %param.20) | copy-start | bytes 49156
  6.5 31.8 %copy-start.7 = (s32[4096]{0:T(1024)S(1)}, s32[4096]{0:T(1024)}, u32[]{:S(2)}) copy-start(s32[4096]{0:T(1024)} %param.21) | copy-start | bytes 49156
  6.5 418.0 %all-gather.3.cloned.1.call-start = ((), (), s32[]{:S(2)}) async-start(), calls=%async_computation | async-start | bytes 1179648 | tf_op jit(solution)/shard_map/all_gather | solution.py:93
  9.9 50.0 %collective-permute-start = (bf16[8,32,1,512]{3,1,2,0:T(8,128)(2,1)S(1)}, bf16[8,32,1,512]{3,1,2,0:T(8,128)(2,1)}, u32[]{:S(2)}, u32[]{:S(2)}) collective-permute-start(bf16[8,32,1,512]{3,1,2,0:T(8,128)(2,1)S(1)} %copy.44), channel_id=1, source_target_pairs={{0,4},{4,8},{8,12},{1,5},{5,9},{9,13},{2,6},{6,10},{10,14},{3,7},{... | collective-permute-start | bytes 786440 | tf_op jit(solution)/shard_map/ppermute | solution.py:20
  16.3 45.0 %collective-permute-start.1 = (bf16[8,32,1,512]{3,1,2,0:T(8,128)(2,1)}, bf16[8,32,1,512]{3,1,2,0:T(8,128)(2,1)}, u32[]{:S(2)}, u32[]{:S(2)}) collective-permute-start(bf16[8,32,1,512]{3,1,2,0:T(8,128)(2,1)} %copy.45), channel_id=1, source_target_pairs={{4,0},{8,4},{12,8},{5,1},{9,5},{13,9},{6,2},{10,6},{14,10},{7,3},{... | collective-permute-start | bytes 786440 | tf_op jit(solution)/shard_map/ppermute | solution.py:22
  36.0 47.4 %copy-start.11 = (f32[512]{0:T(512)}, f32[512]{0:T(512)S(1)}, u32[]{:S(2)}) copy-start(f32[512]{0:T(512)S(1)} %select_multiply_fusion) | copy-start | bytes 6148
  131.2 41.4 %copy-start.9 = (f32[8]{0:T(128)S(1)}, f32[8]{0:T(128)}, u32[]{:S(2)}) copy-start(f32[8]{0:T(128)} %param.13) | copy-start | bytes 100
  131.2 41.4 %slice-start = ((f32[512]{0:T(512)}), f32[128]{0:T(128)S(1)}, s32[]{:S(2)}) async-start(f32[512]{0:T(512)} %copy-done.11), calls=%async_computation.1 | async-start | bytes 1024 | tf_op jit(solution)/shard_map/slice | solution.py:83
  167.8 4.9 %copy-start.2 = (f32[32,64,512]{2,1,0:T(8,128)S(1)}, f32[32,64,512]{2,1,0:T(8,128)}, u32[]{:S(2)}) copy-start(f32[32,64,512]{2,1,0:T(8,128)} %convert_element_type.28) | copy-start | bytes 12582916
  172.7 73.2 %copy-start.12 = (f32[256]{0:T(256)S(1)}, f32[256]{0:T(256)}, u32[]{:S(2)}) copy-start(f32[256]{0:T(256)} %fusion.80) | copy-start | bytes 3076
  330.5 33.5 %copy-start.5 = (s32[4096]{0:T(1024)S(1)}, s32[4096]{0:T(1024)}, u32[]{:S(2)}) copy-start(s32[4096]{0:T(1024)} %broadcast_clamp_fusion) | copy-start | bytes 49156
  330.5 99.8 %copy-start.1 = (f32[64,64]{1,0:T(8,128)S(1)}, f32[64,64]{1,0:T(8,128)}, u32[]{:S(2)}) copy-start(f32[64,64]{1,0:T(8,128)} %param.19) | copy-start | bytes 49156
  364.0 32.3 %copy-start.3 = (f32[4096,32]{0,1:T(8,128)S(1)}, f32[4096,32]{0,1:T(8,128)}, u32[]{:S(2)}) copy-start(f32[4096,32]{0,1:T(8,128)} %copy.39) | copy-start | bytes 1572868
  364.0 32.3 %copy-start.10 = (pred[4096]{0:T(1024)(128)(4,1)S(1)}, pred[4096]{0:T(1024)(128)(4,1)}, u32[]{:S(2)}) copy-start(pred[4096]{0:T(1024)(128)(4,1)} %compare_and_fusion.1) | copy-start | bytes 12292
  364.0 35.9 %copy-start.4 = (s32[4096]{0:T(1024)S(1)}, s32[4096]{0:T(1024)}, u32[]{:S(2)}) copy-start(s32[4096]{0:T(1024)} %param.23) | copy-start | bytes 49156
Sparse Core Ops, SparseCore 0:
  400.0 24.4 all-gather.2
